TPU v7x, 512 devices: a whole 4x4x16 slice. The times are simulated.
512 devices in a mesh: row: 32 (over z, core), col: 16 (over y, x).
Axes of the slice: x: 4, y: 4, z: 16, core: 2. Of those that a mesh axis runs over, the one named last changes fastest.
Arguments:
- tokens: bfloat16 [512, 8192], P('row', 'col'), may hold values from -6 to 6
- out_grad: bfloat16 [512, 8192], P('row', 'col'), may hold values from -1.5 to 1.5
- gate_weight: bfloat16 [8192, 16384], P('col', 'row'), may hold values from -0.0625 to 0.0625
- up_weight: bfloat16 [8192, 16384], P('col', 'row'), may hold values from -0.0625 to 0.0625
- down_weight: bfloat16 [16384, 8192], P('row', 'col'), may hold values from -0.046875 to 0.046875
Outputs:
- input_grad: bfloat16 [512, 8192], P('row', 'col')
- gate_weight_grad: bfloat16 [8192, 16384], P('col', 'row')
- up_weight_grad: bfloat16 [8192, 16384], P('col', 'row')
- down_weight_grad: bfloat16 [16384, 8192], P('row', 'col')
All inputs are finite; a program needn't handle non-finite values.
Results may differ from a plain program's by a relative error of at most 0.005.
Values may be sent and summed in bfloat16 or wider, within the bound.
No kernel may reach another device: no remote copies, remote signals or barrier semaphores. Data moves between devices by JAX's collectives and lax.ppermute only.
A program may use at most 64 MiB of HBM per device.

v0:
```python
import jax
import jax.numpy as jnp
from jax import lax
from jax.sharding import PartitionSpec as P


def pointwise(gate, up, hidden_grad):
    sig = jax.nn.sigmoid(gate)
    act = gate * sig
    hidden = (act * up).astype(jnp.bfloat16)
    gate_grad = (hidden_grad * up * sig * (1.0 + gate * (1.0 - sig))).astype(jnp.bfloat16)
    up_grad = (hidden_grad * act).astype(jnp.bfloat16)
    return (hidden, gate_grad, up_grad)


def body(tokens, out_grad, gate_weight, up_weight, down_weight):
    rows_all, grads_all = (
        lax.all_gather(tokens, "row", axis=0, tiled=True),
        lax.all_gather(out_grad, "row", axis=0, tiled=True),
    )
    contract_cols = (((1,), (1,)), ((), ()))
    contract_rows = (((0,), (0,)), ((), ()))
    gate_part = jnp.dot(rows_all, gate_weight, preferred_element_type=jnp.float32)
    up_part = jnp.dot(rows_all, up_weight, preferred_element_type=jnp.float32)
    grad_part = lax.dot_general(
        grads_all, down_weight, contract_cols, preferred_element_type=jnp.float32
    )
    gate, up, hidden_grad = lax.psum((gate_part, up_part, grad_part), "col")
    hidden, gate_grad, up_grad = pointwise(gate, up, hidden_grad)
    gate_weight_grad = lax.dot_general(
        rows_all, gate_grad, contract_rows, preferred_element_type=jnp.float32
    ).astype(jnp.bfloat16)
    up_weight_grad = lax.dot_general(
        rows_all, up_grad, contract_rows, preferred_element_type=jnp.float32
    ).astype(jnp.bfloat16)
    down_weight_grad = lax.dot_general(
        hidden, grads_all, contract_rows, preferred_element_type=jnp.float32
    ).astype(jnp.bfloat16)
    total = lax.dot_general(
        gate_grad, gate_weight, contract_cols, preferred_element_type=jnp.float32
    )
    input_grad = lax.psum_scatter(
        total
        + lax.dot_general(up_grad, up_weight, contract_cols, preferred_element_type=jnp.float32),
        "row",
        scatter_dimension=0,
        tiled=True,
    )
    return (input_grad.astype(jnp.bfloat16), gate_weight_grad, up_weight_grad, down_weight_grad)


def solution(mesh):
    return jax.shard_map(
        body,
        mesh=mesh,
        in_specs=(
            P("row", "col"),
            P("row", "col"),
            P("col", "row"),
            P("col", "row"),
            P("row", "col"),
        ),
        out_specs=(P("row", "col"), P("col", "row"), P("col", "row"), P("row", "col")),
        check_vma=False,
    )
```

profile of v0, /device:TPU:2, one launch (start us, length us, event | category | flops | bytes accessed | tf_op | source)
XLA Modules:
  0.0 323.2 jit_solution(6330237184376752438)
XLA Ops:
  7.2 0.0 copy-start
  7.2 0.0 copy-start.4
  7.2 0.0 all-reduce.3.cloned.1.call-start
  7.2 38.0 %all_gather.7 = bf16[512,512]{1,0:T(8,128)(2,1)S(1)} all-gather(bf16[16,512]{1,0:T(8,128)(2,1)} %param.5), channel_id=1, replica_groups=mesh['row'=32,'col'=16] {'row'}, dimensions={0}, use_global_device_ids=true | all-gather | bytes 540672 | tf_op jit(solution)/shard_map/all_gather | solution.py:18
  45.3 0.0 copy-done.4
  45.3 28.5 %all_gather.6 = bf16[512,512]{1,0:T(8,128)(2,1)S(1)} all-gather(bf16[16,512]{1,0:T(8,128)(2,1)S(1)} %copy-done.4), channel_id=1, replica_groups=mesh['row'=32,'col'=16] {'row'}, dimensions={0}, use_global_device_ids=true | all-gather | bytes 540672 | tf_op jit(solution)/shard_map/all_gather | solution.py:19
  73.8 0.0 copy-done
  73.8 0.0 copy-start.1
  73.8 1.4 fusion.7
  75.2 0.0 copy-done.1
  75.2 0.0 copy-start.3
  75.2 1.4 fusion.6
  76.7 0.0 copy-done.3
  76.7 1.4 fusion.5
  78.1 0.0 all-reduce.3.cloned.1.call-update
  78.1 0.0 reduce-scatter.2.cloned.1.call-start
  78.2 122.5 %all-reduce.3.cloned.1.call-done = (f32[512,512]{1,0:T(8,128)}, f32[512,512]{1,0:T(8,128)}, f32[512,512]{1,0:T(8,128)}) async-done(((f32[512,512]{1,0:T(8,128)}, f32[512,512]{1,0:T(8,128)}, f32[512,512]{1,0:T(8,128)}), (f32[512,512]{1,0:T(8,128)}, f32[512,512]{1,0:T(8,128)}, f32[512,512]{1,0:T(8,128)})) %all-reduce.3.cloned.1.call-update) | async-done | bytes 3145744 | tf_op jit(solution)/shard_map/psum | solution.py:28
  200.7 2.5 multiply_convert_fusion.1
  203.1 0.5 fusion.8
  203.6 1.5 convolution_add_fusion
  205.1 0.0 reduce-scatter.2.cloned.1.call-update
  205.1 0.5 fusion
  205.5 1.0 copy.9
  206.6 0.5 fusion.1
  207.0 0.0 copy-start.2
  207.0 1.0 copy.10
  208.0 0.4 copy-done.2
  208.4 2.5 convolution_convert_fusion
  211.0 104.1 %reduce-scatter.2.cloned.1.call-done = f32[16,512]{1,0:T(8,128)} async-done(((f32[512,512]{1,0:T(8,128)}), f32[16,512]{1,0:T(8,128)}) %reduce-scatter.2.cloned.1.call-update) | async-done | bytes 32784 | tf_op jit(solution)/shard_map/reduce_scatter | solution.py:42
  315.0 1.4 convert_element_type.29
Async XLA Ops:
  7.2 66.6 %copy-start = (bf16[512,512]{1,0:T(8,128)(2,1)S(1)}, bf16[512,512]{1,0:T(8,128)(2,1)}, u32[]{:S(2)}) copy-start(bf16[512,512]{1,0:T(8,128)(2,1)} %param.7) | copy-start | bytes 1572868
  7.2 38.1 %copy-start.4 = (bf16[16,512]{1,0:T(8,128)(2,1)S(1)}, bf16[16,512]{1,0:T(8,128)(2,1)}, u32[]{:S(2)}) copy-start(bf16[16,512]{1,0:T(8,128)(2,1)} %param.6) | copy-start | bytes 49156
  7.2 193.5 %all-reduce.3.cloned.1.call-start = ((), (), s32[]{:S(2)}) async-start(), calls=%async_computation.2 | async-start | bytes 6291456 | tf_op jit(solution)/shard_map/psum | solution.py:28
  73.8 1.4 copy-start.1
  75.2 1.5 copy-start.3
  78.1 236.9 %reduce-scatter.2.cloned.1.call-start = ((), (), s32[]{:S(2)}) async-start(), calls=%async_computation.1 | async-start | bytes 1081344 | tf_op jit(solution)/shard_map/reduce_scatter | solution.py:42
  207.0 1.4 copy-start.2
Sparse Core Ops, SparseCore 0:
  78.2 122.3 all-reduce.2
  205.2 109.7 reduce-scatter.1
where the time goes:
time: 324 us; the launch traced here: 323 us
  waiting for transfers between devices  227 us (70%)
  blocking collectives  66.5 us (21%)
  between operations  14.1 us (4%)
  matrix products  9.67 us (3%)
  other arithmetic  3.82 us (1%)
    psum x1, waiting for transfers between devices, body(): gate, up, hidden_grad = lax.psum((gate_part, up_part, grad_part), 'col')  122 us
    reduce_scatter x1, waiting for transfers between devices, body(): lax.psum_scatter(total + lax.dot_general(up_grad, up_weight, contract_col...  104 us
    all_gather x1, blocking collectives, body(): lax.all_gather(tokens, 'row', axis=0, tiled=True)  38 us
    all_gather x1, blocking collectives, body(): lax.all_gather(out_grad, 'row', axis=0, tiled=True)  28.5 us
  transfers between devices with their start and end apart: 2, of which 2 were waited for; matrix products, arithmetic and copies ran while one was open for 2% of the time, Pallas kernels for 0%

commit v1 on v0

--- a/solution.py
+++ b/solution.py
@@ -15,7 +15,9 @@
 
 def body(tokens, out_grad, gate_weight, up_weight, down_weight):
     rows_all, grads_all = (
-        lax.all_gather(tokens, "row", axis=0, tiled=True),
+        jnp.concatenate(
+            lax.all_to_all(jnp.stack([tokens] * lax.axis_size("row")), "row", 0, 0), axis=0
+        ),
         lax.all_gather(out_grad, "row", axis=0, tiled=True),
     )
     contract_cols = (((1,), (1,)), ((), ()))

time: 324 us -> 329 us (1.015)
  starting transfers between devices: 0.08 us -> 15.7 us
  blocking collectives: 66.5 us -> 51.1 us
    all_gather x1 -> x0, blocking collectives: 38 us -> none  [body(): lax.all_gather(tokens, 'row', axis=0, tiled=True)]
    all_gather x1, blocking collectives: 28.5 us -> 51.1 us  [body(): lax.all_gather(out_grad, 'row', axis=0, tiled=True)]
    all_to_all x0 -> x1, starting transfers between devices: none -> 15.6 us  [body(): lax.all_to_all(jnp.stack([tokens] * lax.axis_size('row')), 'row', 0, 0)]
  transfers between devices with their start and end apart: 2 -> 3, of which waited for: 2 -> 2; matrix products, arithmetic and copies ran while one was open for 2% -> 2% of each run, Pallas kernels for 0% -> 0%
where the time goes in v1:
time: 329 us; the launch traced here: 328 us
  waiting for transfers between devices  230 us (70%)
  blocking collectives  51.1 us (16%)
  starting transfers between devices  15.7 us (5%)
  between operations  14.1 us (4%)
  matrix products  9.68 us (3%)
  local copies, waits for them, and re-layouts  4.06 us (1%)
  other arithmetic  3.82 us (1%)
    psum x1, waiting for transfers between devices, body(): gate, up, hidden_grad = lax.psum((gate_part, up_part, grad_part), 'col')  126 us
    reduce_scatter x1, waiting for transfers between devices, body(): lax.psum_scatter(total + lax.dot_general(up_grad, up_weight, contract_col...  104 us
    all_gather x1, blocking collectives, body(): lax.all_gather(out_grad, 'row', axis=0, tiled=True)  51.1 us
    all_to_all x1, starting transfers between devices, body(): lax.all_to_all(jnp.stack([tokens] * lax.axis_size('row')), 'row', 0, 0)  15.6 us
  transfers between devices with their start and end apart: 3, of which 2 were waited for; matrix products, arithmetic and copies ran while one was open for 2% of the time, Pallas kernels for 0%

profile of v1, /device:TPU:2, one launch (start us, length us, event | category | flops | bytes accessed | tf_op | source)
XLA Modules:
  0.0 328.1 jit_solution(4223333563694570269)
XLA Ops:
  7.2 0.0 copy-start
  7.2 1.6 stack.2
  8.8 0.0 copy-start.4
  8.8 15.6 %all-to-all-start = ((bf16[32,16,512]{2,1,0:T(8,128)(2,1)}), bf16[32,16,512]{2,1,0:T(8,128)(2,1)S(1)}, u32[]{:S(2)}, u32[]{:S(2)}) async-start(bf16[32,16,512]{2,1,0:T(8,128)(2,1)} %stack.2), calls=%async_computation | async-start | bytes 1048576 | tf_op jit(solution)/shard_map/all_to_all | solution.py:19
  24.4 0.0 copy-start.3
  24.4 0.0 all-reduce.3.cloned.1.call-start
  24.5 0.0 copy-done.4
  24.5 51.1 %all_gather.3 = bf16[512,512]{1,0:T(8,128)(2,1)S(1)} all-gather(bf16[16,512]{1,0:T(8,128)(2,1)S(1)} %copy-done.4), channel_id=1, replica_groups=mesh['row'=32,'col'=16] {'row'}, dimensions={0}, use_global_device_ids=true | all-gather | bytes 540672 | tf_op jit(solution)/shard_map/all_gather | solution.py:21
  75.6 0.0 copy-done.3
  75.6 1.4 fusion.5
  77.1 0.0 all-to-all-done
  77.1 0.0 copy-done
  77.1 0.0 copy-start.1
  77.1 1.4 fusion.7
  78.5 0.0 copy-done.1
  78.5 1.4 fusion.6
  79.9 0.0 all-reduce.3.cloned.1.call-update
  80.0 0.0 reduce-scatter.2.cloned.1.call-start
  80.0 125.5 %all-reduce.3.cloned.1.call-done = (f32[512,512]{1,0:T(8,128)}, f32[512,512]{1,0:T(8,128)}, f32[512,512]{1,0:T(8,128)}) async-done(((f32[512,512]{1,0:T(8,128)}, f32[512,512]{1,0:T(8,128)}, f32[512,512]{1,0:T(8,128)}), (f32[512,512]{1,0:T(8,128)}, f32[512,512]{1,0:T(8,128)}, f32[512,512]{1,0:T(8,128)})) %all-reduce.3.cloned.1.call-update) | async-done | bytes 3145744 | tf_op jit(solution)/shard_map/psum | solution.py:30
  205.5 2.5 multiply_convert_fusion.1
  208.0 0.5 fusion.8
  208.5 1.5 convolution_add_fusion
  209.9 0.0 reduce-scatter.2.cloned.1.call-update
  209.9 0.5 fusion
  210.4 1.0 copy.9
  211.4 0.5 fusion.1
  211.9 0.0 copy-start.2
  211.9 1.0 copy.10
  212.9 0.4 copy-done.2
  213.3 2.5 convolution_convert_fusion
  215.8 104.1 %reduce-scatter.2.cloned.1.call-done = f32[16,512]{1,0:T(8,128)} async-done(((f32[512,512]{1,0:T(8,128)}), f32[16,512]{1,0:T(8,128)}) %reduce-scatter.2.cloned.1.call-update) | async-done | bytes 32784 | tf_op jit(solution)/shard_map/reduce_scatter | solution.py:44
  319.9 1.4 convert_element_type.29
Async XLA Ops:
  7.2 69.9 %copy-start = (bf16[512,512]{1,0:T(8,128)(2,1)S(1)}, bf16[512,512]{1,0:T(8,128)(2,1)}, u32[]{:S(2)}) copy-start(bf16[512,512]{1,0:T(8,128)(2,1)} %param.7) | copy-start | bytes 1572868
  8.8 15.7 %copy-start.4 = (bf16[16,512]{1,0:T(8,128)(2,1)S(1)}, bf16[16,512]{1,0:T(8,128)(2,1)}, u32[]{:S(2)}) copy-start(bf16[16,512]{1,0:T(8,128)(2,1)} %param.6) | copy-start | bytes 49156
  8.8 68.2 %all-to-all-start = ((bf16[32,16,512]{2,1,0:T(8,128)(2,1)}), bf16[32,16,512]{2,1,0:T(8,128)(2,1)S(1)}, u32[]{:S(2)}, u32[]{:S(2)}) async-start(bf16[32,16,512]{2,1,0:T(8,128)(2,1)} %stack.2), calls=%async_computation | async-start | bytes 1048576 | tf_op jit(solution)/shard_map/all_to_all | solution.py:19
  24.4 51.2 %copy-start.3 = (bf16[512,512]{1,0:T(8,128)(2,1)S(1)}, bf16[512,512]{1,0:T(8,128)(2,1)}, u32[]{:S(2)}) copy-start(bf16[512,512]{1,0:T(8,128)(2,1)} %param.9) | copy-start | bytes 1572868
  24.4 181.1 %all-reduce.3.cloned.1.call-start = ((), (), s32[]{:S(2)}) async-start(), calls=%async_computation.3 | async-start | bytes 6291456 | tf_op jit(solution)/shard_map/psum | solution.py:30
  77.1 1.4 copy-start.1
  80.0 240.0 %reduce-scatter.2.cloned.1.call-start = ((), (), s32[]{:S(2)}) async-start(), calls=%async_computation.2 | async-start | bytes 1081344 | tf_op jit(solution)/shard_map/reduce_scatter | solution.py:44
  211.9 1.4 copy-start.2
Sparse Core Ops, SparseCore 0:
  80.1 125.4 all-reduce.2
  210.1 109.8 reduce-scatter.1
